TPU v7x, 32 devices: a whole 2x2x4 slice. The times are simulated.
32 devices in a mesh: bl: 4 (over y, x), freq: 8 (over z, core).
Axes of the slice: x: 2, y: 2, z: 4, core: 2. Of those that a mesh axis runs over, the one named last changes fastest.
Arguments:
- visibility: bfloat16 [2, 64, 1024, 4096], P(None, None, 'freq', 'bl'), may hold values from -6 to 6
- mode_index: int32 [256], replicated, may hold values from 0 to 2047
- beam_mode_weights: bfloat16 [256, 64, 64], replicated, may hold values from -0.75 to 0.75
- inverse_cov: float32 [256, 1024, 1024], P(('bl', 'freq')), may hold values from -2 to 3, as said below
- noise_power: float32 [256, 1024], P(('bl', 'freq')), may hold values from 0.2 to 2
Outputs:
- filtered: float32 [256, 1024, 128], P(('bl', 'freq'))
Inputs may be any that keep to these rules, and one draw needn't show every extreme that they name: Each inverse_cov[m] is symmetric positive definite.
All inputs are finite; a program needn't handle non-finite values.
Results may differ from a plain program's by a relative error of at most 0.0023.
Values may be sent and summed in bfloat16 or wider, within the bound.
No kernel may reach another device: no remote copies, remote signals or barrier semaphores. Data moves between devices by JAX's collectives and lax.ppermute only.
A program may use at most 192 MiB of HBM per device.

v0:
```python
import math
import jax
import jax.numpy as jnp
from jax import lax
from jax.sharding import PartitionSpec as P


def dft_table(mode_index, sample_ids, length):
    phase_steps = mode_index[None, :] * sample_ids[:, None] % length
    phases = phase_steps.astype(jnp.float32) * (2.0 * math.pi / length)
    norming = 1.0 / math.sqrt(length)
    cosine = jnp.cos(phases) * norming
    sine_part = jnp.sin(phases) * norming
    real_rows = jnp.concatenate([cosine, -sine_part], axis=1)
    imag_rows = jnp.concatenate([sine_part, cosine], axis=1)
    return jnp.stack([real_rows, imag_rows]).astype(jnp.bfloat16)


def transform(samples, dft_weights):
    return lax.dot_general(
        samples, dft_weights, (((0, 3), (0, 1)), ((), ())), preferred_element_type=jnp.float32
    )


def project(spectrum, beam_rows):
    row_count, freq_count, column_total = spectrum.shape
    mode_count = column_total // 2
    halves = spectrum.reshape(row_count, freq_count, 2, mode_count)
    projected = jnp.einsum(
        "bfcm,msb->mfcs", halves, beam_rows.astype(jnp.float32), precision=lax.Precision.HIGHEST
    )
    return projected.reshape(mode_count, freq_count, 2 * beam_rows.shape[1])


def weigh_all(inverse_cov, noise_power, owner_modes):
    weighted = jnp.einsum("mfg,mgk->mfk", inverse_cov, owner_modes, precision=lax.Precision.HIGHEST)
    return owner_modes - noise_power[:, :, None] * weighted


def body(visibility, mode_index, beam_mode_weights, inverse_cov, noise_power):
    bl_devices = lax.axis_size("bl")
    local_times = visibility.shape[3]
    total_times = local_times * bl_devices
    sample_ids = lax.axis_index("bl") * local_times + jnp.arange(local_times, dtype=jnp.int32)
    dft_weights = dft_table(mode_index, sample_ids, total_times)
    partial_terms = project(transform(visibility, dft_weights), beam_mode_weights)
    summed_modes = lax.psum_scatter(partial_terms, "bl", scatter_dimension=0, tiled=True)
    owner_modes = lax.all_to_all(summed_modes, "freq", split_axis=0, concat_axis=1, tiled=True)
    return weigh_all(inverse_cov, noise_power, owner_modes)


def solution(mesh):
    placed = (
        P(None, None, "freq", "bl"),
        P(),
        P(),
        P(("bl", "freq"), None, None),
        P(("bl", "freq"), None),
    )
    return jax.shard_map(
        body, mesh=mesh, in_specs=placed, out_specs=P(("bl", "freq"), None, None), check_vma=False
    )
```

profile of v0, /device:TPU:0, one launch (start us, length us, event | category | flops | bytes accessed | tf_op | source)
XLA Modules:
  0.0 386.1 jit_solution(9053859770540490229)
XLA Ops:
  6.5 0.0 copy-start.2
  6.5 0.0 reduce-scatter.2.cloned.1.call-start
  6.5 7.4 %copy.12 = bf16[256,64,64,1]{2,1,3,0:T(8,128)(2,1)} copy(bf16[256,64,64,1]{0,2,1,3:T(8,128)(2,1)} %bitcast.37) | data formatting | bytes 4194304 | tf_op args[2]
  14.0 0.0 copy-done.2
  14.0 4.6 %negate_convert_fusion = (bf16[1024,256]{0,1:T(8,128)(2,1)S(1)}, bf16[1024,256]{0,1:T(8,128)(2,1)S(1)}, bf16[1024,256]{0,1:T(8,128)(2,1)S(1)}) fusion(s32[1024]{0:T(1024)S(1)} %iota_add_fusion, s32[256]{0:T(256)S(1)} %copy-done.2), kind=kLoop, calls=%fused_computation.19 | loop fusion | flops 5242880 | bytes 1577984 | tf_op jit(solution)/shard_map/convert.7
  18.5 0.3 maximum_bitcast_fusion
  18.8 0.0 copy-start
  18.8 24.1 %fusion.2 = f32[512,64,128,1]{2,0,1,3:T(8,128)} fusion(bf16[2,64,128,1024]{3,2,1,0:T(8,128)(2,1)} %param.5, bf16[1,1024,512]{1,2,0:T(8,128)(2,1)S(1)} %get-tuple-element.6, bf16[1,1024,512]{1,2,0:T(8,128)(2,1)S(1)} %get-tuple-element.5), kind=kOutput, calls=%fused_computation.4 | convolution fusion | flops 17184063488 | bytes 52428800 | tf_op jit(solution)/shard_map/dot_general | solution.py:20
  42.9 0.0 copy-done
  42.9 26.9 %fusion = f32[256,128,2,64]{1,3,2,0:T(8,128)} fusion(bf16[256,64,64,1]{2,1,3,0:T(8,128)(2,1)S(1)} %copy-done, f32[64,128,2,256]{1,3,2,0:T(8,128)} %bitcast.34), kind=kOutput, calls=%fused_computation | convolution fusion | flops 3221225472 | bytes 35651584 | tf_op jit(solution)/shard_map/bfcm,msb->mfcs/dot_general | solution.py:29
  69.8 0.0 reduce-scatter.2.cloned.1.call-update
  69.8 156.7 %reduce-scatter.2.cloned.1.call-done = f32[64,128,128]{1,2,0:T(8,128)} async-done(((f32[256,128,128]{1,2,0:T(8,128)}), f32[64,128,128]{1,2,0:T(8,128)}) %reduce-scatter.2.cloned.1.call-update) | async-done | bytes 4194320 | tf_op jit(solution)/shard_map/reduce_scatter | solution.py:47
  226.5 98.6 %all_to_all.18 = f32[64,128,128]{1,2,0:T(8,128)S(1)} all-to-all(f32[64,128,128]{1,2,0:T(8,128)} %reduce-scatter.2.cloned.1.call-done), channel_id=1, replica_groups=mesh['bl'=4,'freq'=8] {'freq'}, dimensions={0} | all-to-all | bytes 8388608 | tf_op jit(solution)/shard_map/all_to_all | solution.py:48
  325.1 4.4 %copy.18 = f32[8,8,128,128]{2,0,3,1:T(8,128)} copy(f32[8,8,128,128]{2,3,1,0:T(8,128)S(1)} %bitcast.35) | data formatting | bytes 8388608 | tf_op jit(solution)/shard_map/all_to_all | solution.py:48
  329.5 0.0 copy-start.1
  329.5 4.9 %all_to_all.16 = f32[8,1024,128]{1,2,0:T(8,128)} reshape(f32[8,8,128,128]{2,1,3,0:T(8,128)} %bitcast.36) | data formatting | bytes 8388608 | tf_op jit(solution)/shard_map/all_to_all | solution.py:48
  334.4 0.0 copy-done.1
  334.4 39.6 %bitcast_subtract_fusion = f32[8,1024,128]{1,2,0:T(8,128)} fusion(f32[8,1024,128]{1,2,0:T(8,128)} %all_to_all.16, f32[8,1024,1024]{2,1,0:T(8,128)} %param.8, f32[8,1024]{1,0:T(8,128)S(1)} %copy-done.1), kind=kOutput, calls=%fused_computation.2 | convolution fusion | flops 12886999040 | bytes 41975808 | tf_op jit(solution)/shard_map/mfg,mgk->mfk/dot_general | solution.py:36
  374.0 5.3 %copy.10 = f32[8,1024,128]{2,1,0:T(8,128)} copy(f32[8,1024,128]{1,2,0:T(8,128)} %bitcast_subtract_fusion) | data formatting | bytes 8388608 | tf_op jit(solution)/shard_map/sub | solution.py:37
  (1 shorter events, 0.0 us)
Async XLA Ops:
  6.5 7.4 %copy-start.2 = (s32[256]{0:T(256)S(1)}, s32[256]{0:T(256)}, u32[]{:S(2)}) copy-start(s32[256]{0:T(256)} %param.6) | copy-start | bytes 3076
  6.5 220.0 %reduce-scatter.2.cloned.1.call-start = ((), (), s32[]{:S(2)}) async-start(), calls=%async_computation.2 | async-start | bytes 20971520 | tf_op jit(solution)/shard_map/reduce_scatter | solution.py:47
  18.8 24.1 %copy-start = (bf16[256,64,64,1]{2,1,3,0:T(8,128)(2,1)S(1)}, bf16[256,64,64,1]{2,1,3,0:T(8,128)(2,1)}, u32[]{:S(2)}) copy-start(bf16[256,64,64,1]{2,1,3,0:T(8,128)(2,1)} %copy.12) | copy-start | bytes 6291460
  329.5 4.9 %copy-start.1 = (f32[8,1024]{1,0:T(8,128)S(1)}, f32[8,1024]{1,0:T(8,128)}, u32[]{:S(2)}) copy-start(f32[8,1024]{1,0:T(8,128)} %param.9) | copy-start | bytes 98308
Sparse Core Ops, SparseCore 0:
  69.9 156.5 reduce-scatter.1
where the time goes:
time: 387 us; the launch traced here: 386 us
  waiting for transfers between devices  157 us (41%)
  blocking collectives  98.6 us (25%)
  matrix products  90.5 us (23%)
  local copies, waits for them, and re-layouts  22 us (6%)
  between operations  13.4 us (3%)
  other arithmetic  4.84 us (1%)
    reduce_scatter x1, waiting for transfers between devices, body(): lax.psum_scatter(partial_terms, 'bl', scatter_dimension=0, tiled=True)  157 us
    all_to_all x1, blocking collectives, body(): lax.all_to_all(summed_modes, 'freq', split_axis=0, concat_axis=1, tiled=T...  98.6 us
    dot_general x1, matrix products, weigh_all(): jnp.einsum('mfg,mgk->mfk', inverse_cov, owner_modes, precision=lax.Precis...  39.6 us
    dot_general x1, matrix products, project(): jnp.einsum('bfcm,msb->mfcs', halves, beam_rows.astype(jnp.float32), preci...  26.9 us
    dot_general x1, matrix products, transform(): lax.dot_general(samples, dft_weights, (((0, 3), (0, 1)), ((), ())), prefe...  24.1 us
    all_to_all x2, local copies, waits for them, and re-layouts, body(): lax.all_to_all(summed_modes, 'freq', split_axis=0, concat_axis=1, tiled=T...  9.26 us
  transfers between devices with their start and end apart: 1, of which 1 were waited for; matrix products, arithmetic and copies ran while one was open for 0% of the time, Pallas kernels for 0%

commit v1 on v0

--- a/solution.py
+++ b/solution.py
@@ -45,7 +45,12 @@
     dft_weights = dft_table(mode_index, sample_ids, total_times)
     partial_terms = project(transform(visibility, dft_weights), beam_mode_weights)
     summed_modes = lax.psum_scatter(partial_terms, "bl", scatter_dimension=0, tiled=True)
-    owner_modes = lax.all_to_all(summed_modes, "freq", split_axis=0, concat_axis=1, tiled=True)
+    owner_modes = jnp.concatenate(
+        lax.all_to_all(
+            jnp.stack(jnp.split(summed_modes, lax.axis_size("freq"), axis=0)), "freq", 0, 0
+        ),
+        axis=1,
+    )
     return weigh_all(inverse_cov, noise_power, owner_modes)
 
 

time: 387 us -> 387 us (level)
    all_to_all x2 -> x0, local copies, waits for them, and re-layouts: 9.26 us -> none  [body(): lax.all_to_all(summed_modes, 'freq', split_axis=0, concat_axis=1, tiled=T...]
    unnamed x7 -> x14, local copies, waits for them, and re-layouts: 7.42 us -> 15 us
where the time goes in v1:
time: 387 us; the launch traced here: 386 us
  waiting for transfers between devices  157 us (41%)
  blocking collectives  98.4 us (25%)
  matrix products  91.6 us (24%)
  local copies, waits for them, and re-layouts  21.4 us (6%)
  between operations  13.5 us (3%)
  other arithmetic  4.84 us (1%)
    reduce_scatter x1, waiting for transfers between devices, body(): lax.psum_scatter(partial_terms, 'bl', scatter_dimension=0, tiled=True)  157 us
    all_to_all x1, blocking collectives, body(): lax.all_to_all(jnp.stack(jnp.split(summed_modes, lax.axis_size('freq'), a...  98.4 us
    dot_general x1, matrix products, weigh_all(): jnp.einsum('mfg,mgk->mfk', inverse_cov, owner_modes, precision=lax.Precis...  40.6 us
    dot_general x1, matrix products, project(): jnp.einsum('bfcm,msb->mfcs', halves, beam_rows.astype(jnp.float32), preci...  26.9 us
    dot_general x1, matrix products, transform(): lax.dot_general(samples, dft_weights, (((0, 3), (0, 1)), ((), ())), prefe...  24.1 us
    unnamed x14, local copies, waits for them, and re-layouts  15 us
  transfers between devices with their start and end apart: 1, of which 1 were waited for; matrix products, arithmetic and copies ran while one was open for 0% of the time, Pallas kernels for 0%

profile of v1, /device:TPU:0, one launch (start us, length us, event | category | flops | bytes accessed | tf_op | source)
XLA Modules:
  0.0 386.4 jit_solution(14885053515185907904)
XLA Ops:
  6.5 0.0 reduce-scatter.2.cloned.1.call-start
  6.5 7.4 %copy.12 = bf16[256,64,64,1]{2,1,3,0:T(8,128)(2,1)} copy(bf16[256,64,64,1]{0,2,1,3:T(8,128)(2,1)} %bitcast.70) | data formatting | bytes 4194304 | tf_op args[2]
  14.0 0.0 copy-done.2
  14.0 4.6 %negate_convert_fusion = (bf16[1024,256]{0,1:T(8,128)(2,1)S(1)}, bf16[1024,256]{0,1:T(8,128)(2,1)S(1)}, bf16[1024,256]{0,1:T(8,128)(2,1)S(1)}) fusion(s32[1024]{0:T(1024)S(1)} %iota_add_fusion, s32[256]{0:T(256)S(1)} %copy-done.2), kind=kLoop, calls=%fused_computation.21 | loop fusion | flops 5242880 | bytes 1577984 | tf_op jit(solution)/shard_map/convert.7
  18.5 0.3 maximum_bitcast_fusion
  18.8 0.0 copy-start
  18.8 24.1 %fusion.7 = f32[512,64,128,1]{2,0,1,3:T(8,128)} fusion(bf16[2,64,128,1024]{3,2,1,0:T(8,128)(2,1)} %param.5, bf16[1,1024,512]{1,2,0:T(8,128)(2,1)S(1)} %get-tuple-element.6, bf16[1,1024,512]{1,2,0:T(8,128)(2,1)S(1)} %get-tuple-element.5), kind=kOutput, calls=%fused_computation.6 | convolution fusion | flops 17184063488 | bytes 52428800 | tf_op jit(solution)/shard_map/dot_general | solution.py:20
  42.9 0.0 copy-done
  42.9 26.9 %fusion = f32[256,128,2,64]{1,3,2,0:T(8,128)} fusion(bf16[256,64,64,1]{2,1,3,0:T(8,128)(2,1)S(1)} %copy-done, f32[64,128,2,256]{1,3,2,0:T(8,128)} %bitcast.69), kind=kOutput, calls=%fused_computation | convolution fusion | flops 3221225472 | bytes 35651584 | tf_op jit(solution)/shard_map/bfcm,msb->mfcs/dot_general | solution.py:29
  69.8 0.0 reduce-scatter.2.cloned.1.call-update
  69.8 156.7 %reduce-scatter.2.cloned.1.call-done = f32[64,128,128]{1,2,0:T(8,128)} async-done(((f32[256,128,128]{1,2,0:T(8,128)}), f32[64,128,128]{1,2,0:T(8,128)}) %reduce-scatter.2.cloned.1.call-update) | async-done | bytes 4194320 | tf_op jit(solution)/shard_map/reduce_scatter | solution.py:47
  226.5 1.1 fusion.23
  227.6 1.1 fusion.22
  228.7 1.1 fusion.21
  229.8 1.1 fusion.20
  230.8 1.1 fusion.19
  231.9 1.1 fusion.18
  233.0 1.1 fusion.17
  234.1 1.1 fusion.16
  235.2 0.0 copy-start.1
  235.2 98.4 %all_to_all.5 = f32[8,8,128,128]{2,3,1,0:T(8,128)S(1)} all-to-all(f32[8,8,128,128]{2,3,1,0:T(8,128)S(1)} %fusion.16), channel_id=1, replica_groups=mesh['bl'=4,'freq'=8] {'freq'}, dimensions={0} | all-to-all | bytes 8388608 | tf_op jit(solution)/shard_map/all_to_all | solution.py:49
  333.6 0.0 copy-done.1
  333.6 40.6 %bitcast_subtract_fusion = f32[8,1024,128]{1,2,0:T(8,128)} fusion(f32[8,1024,1024]{2,1,0:T(8,128)} %param.8, f32[8,1024]{1,0:T(8,128)S(1)} %copy-done.1, f32[8,8,128,128]{2,3,1,0:T(8,128)S(1)} %all_to_all.5), kind=kOutput, calls=%fused_computation.2 | convolution fusion | flops 12886999040 | bytes 41975808 | tf_op jit(solution)/shard_map/mfg,mgk->mfk/dot_general | solution.py:36
  374.2 5.3 %copy.10 = f32[8,1024,128]{2,1,0:T(8,128)} copy(f32[8,1024,128]{1,2,0:T(8,128)} %bitcast_subtract_fusion) | data formatting | bytes 8388608 | tf_op jit(solution)/shard_map/sub | solution.py:37
  (2 shorter events, 0.0 us)
Async XLA Ops:
  6.5 7.4 %copy-start.2 = (s32[256]{0:T(256)S(1)}, s32[256]{0:T(256)}, u32[]{:S(2)}) copy-start(s32[256]{0:T(256)} %param.6) | copy-start | bytes 3076
  6.5 220.0 %reduce-scatter.2.cloned.1.call-start = ((), (), s32[]{:S(2)}) async-start(), calls=%async_computation.2 | async-start | bytes 20971520 | tf_op jit(solution)/shard_map/reduce_scatter | solution.py:47
  18.8 24.1 %copy-start = (bf16[256,64,64,1]{2,1,3,0:T(8,128)(2,1)S(1)}, bf16[256,64,64,1]{2,1,3,0:T(8,128)(2,1)}, u32[]{:S(2)}) copy-start(bf16[256,64,64,1]{2,1,3,0:T(8,128)(2,1)} %copy.12) | copy-start | bytes 6291460
  235.2 98.4 %copy-start.1 = (f32[8,1024]{1,0:T(8,128)S(1)}, f32[8,1024]{1,0:T(8,128)}, u32[]{:S(2)}) copy-start(f32[8,1024]{1,0:T(8,128)} %param.9) | copy-start | bytes 98308
Sparse Core Ops, SparseCore 0:
  69.9 156.5 reduce-scatter.1
